TPU v7x, 32 devices: a whole 2x2x4 slice. The times are simulated.
32 devices in a mesh: dp: 8 (over z, x), fsdp: 4 (over y, core).
Axes of the slice: x: 2, y: 2, z: 4, core: 2. Of those that a mesh axis runs over, the one named last changes fastest.
Arguments:
- dec_hidden: bfloat16 [1024, 4096], P('dp'), may hold values from -18 to 18
- w_query: bfloat16 [4096, 2048], P(None, 'fsdp'), may hold values from -0.01171875 to 0.01171875
- enc_states: bfloat16 [2, 1536, 2048], P(None, 'dp', 'fsdp')
- w_out: bfloat16 [2048, 4096], P('fsdp'), may hold values from -0.5 to 0.5
- norm_gain: float32 [4096], replicated, may hold values from 0.25 to 1.75
- w_vocab: bfloat16 [4096, 16384], P(None, 'fsdp'), may hold values from -1 to 1
- enc_segment: int32 [1536], replicated, may hold values from 0 to 3, as said below
- dec_segment: int32 [1024], P('dp'), may hold values from 0 to 3, as said below
- seg_map: int32 [8, 4], replicated, may hold values from 0 to 31, as said below
- targets: int32 [1024], P('dp'), may hold values from 0 to 16383
- loss_mask: int32 [1024], P('dp'), may hold values from 0 to 1, as said below
Outputs:
- mean_loss: float32 [], replicated
- grad_hidden: bfloat16 [1024, 4096], P('dp', 'fsdp')
- grad_gain: float32 [4096], P('fsdp')
Inputs may be any that keep to these rules, and one draw needn't show every extreme that they name: `enc_segment`: each encoder row of 192 tokens holds 4 segments numbered in order, never falling, each nonempty and at most 80 tokens long; one segment of every row is exactly 80 long. `dec_segment`: each decoder row of 128 tokens holds 4 segments numbered in order, never falling, each nonempty and at most 56 tokens long; one segment of every row is exactly 56 long. seg_map[b, j] names the encoder segment (encoder row times 4 plus its number in that row) read by segment j of decoder row b. Every encoder segment is named exactly once. The encoder row read in column j is (b + o_j) mod 8, with offsets o_j that are the same for every decoder row and differ between columns; one of them is 4 and one is 7. The segments of one encoder row go to different decoder rows. `loss_mask`: the first token of every decoder row has mask 1.
All inputs are finite; a program needn't handle non-finite values.
Results may differ from a plain program's by a relative error of at most 0.0086.
Values may be sent and summed in bfloat16 or wider, within the bound.
No kernel may reach another device: no remote copies, remote signals or barrier semaphores. Data moves between devices by JAX's collectives and lax.ppermute only.
A program may use at most 128 MiB of HBM per device.

v0:
```python
import jax
import jax.numpy as jnp
from jax import lax
from jax.sharding import PartitionSpec as P

HEAD_DIM = 64


def joined(x, axis, combine):
    everything = jax.tree.map(lambda part: lax.all_gather(part, axis), x)
    leading = jax.tree.map(lambda part: part[0], everything)

    def turn(k, so_far):
        return combine(so_far, jax.tree.map(lambda part: part[k], everything))

    return lax.fori_loop(1, lax.axis_size(axis), turn, leading)


def merge_totals(first_set, second_set):
    larger = jnp.maximum(first_set[0], second_set[0])
    combined = first_set[1] * jnp.exp(first_set[0] - larger) + second_set[1] * jnp.exp(
        second_set[0] - larger
    )
    return (larger, combined, first_set[2] + second_set[2])


def attend(carry, block, block_ids, queries, sources):
    run_max, run_sum, run_acc = carry
    block_rows = block.shape[1]
    heads_here = queries.shape[1]
    keys_block = block[0].astype(jnp.float32).reshape(block_rows, heads_here, HEAD_DIM)
    values_block = block[1].astype(jnp.float32).reshape(block_rows, heads_here, HEAD_DIM)
    scores = jnp.einsum("ihd,jhd->hij", queries, keys_block)
    allowed = (sources[:, None] == block_ids[None, :])[None]
    new_max = jnp.maximum(run_max, jnp.max(jnp.where(allowed, scores, jnp.float32(-1e30)), 2))
    weights = jnp.where(allowed, jnp.exp(scores - new_max[:, :, None]), 0.0)
    run_sum = jnp.sum(weights, 2)
    run_acc = jnp.einsum("hij,jhd->hid", weights, values_block)
    return (new_max, run_sum, run_acc)


def body(
    dec_hidden,
    w_query,
    enc_states,
    w_out,
    norm_gain,
    w_vocab,
    enc_segment,
    dec_segment,
    seg_map,
    targets,
    loss_mask,
):
    dp_index = lax.axis_index("dp")
    fsdp_index = lax.axis_index("fsdp")
    dp_count = lax.axis_size("dp")
    dec_len, width = dec_hidden.shape
    enc_len = enc_states.shape[1]
    heads_here = w_query.shape[1] // HEAD_DIM
    segments = seg_map.shape[1]
    feature_count = width // lax.axis_size("fsdp")
    vocab_here = w_vocab.shape[1]
    map_row = lax.dynamic_index_in_dim(seg_map, dp_index, 0, keepdims=False)
    segment_picks = dec_segment[:, None] == jnp.arange(segments)[None, :]
    sources = jnp.sum(jnp.where(segment_picks, map_row[None, :], 0), 1)
    query_proj = jnp.dot(dec_hidden, w_query, preferred_element_type=jnp.float32).astype(
        jnp.bfloat16
    )
    queries = (
        lax.optimization_barrier(query_proj)
        .astype(jnp.float32)
        .reshape(dec_len, heads_here, HEAD_DIM)
    )
    start_state = (
        jnp.full((heads_here, dec_len), -1e30, jnp.float32),
        jnp.zeros((heads_here, dec_len), jnp.float32),
        jnp.zeros((heads_here, dec_len, HEAD_DIM), jnp.float32),
    )
    global_ids = jnp.arange(dp_count * enc_len) // enc_len * segments + enc_segment
    state = attend(
        start_state,
        lax.all_gather(enc_states, "dp", axis=1, tiled=True),
        global_ids,
        queries,
        sources,
    )
    run_max, run_sum, run_acc = state
    attended = (
        (run_acc / run_sum[:, :, None])
        .transpose(1, 0, 2)
        .reshape(dec_len, heads_here * HEAD_DIM)
        .astype(jnp.bfloat16)
    )
    feature_start = fsdp_index * feature_count
    gain_part = lax.dynamic_slice_in_dim(norm_gain, feature_start, feature_count, 0)
    summed_full = lax.psum(
        jnp.dot(attended, w_out, preferred_element_type=jnp.float32), "fsdp"
    ) + dec_hidden.astype(jnp.float32)
    inv_root = lax.rsqrt(jnp.sum(summed_full * summed_full, 1) / width + 1e-06)
    unit_full = summed_full * inv_root[:, None]
    normed_full = (unit_full * norm_gain).astype(jnp.bfloat16)
    logits = jnp.dot(normed_full, w_vocab, preferred_element_type=jnp.float32)
    unit_part = lax.dynamic_slice_in_dim(unit_full, feature_start, feature_count, 1)
    local_target = targets - fsdp_index * vocab_here
    picked = jnp.arange(vocab_here)[None, :] == local_target[:, None]
    local_top = jnp.max(logits, 1)
    local_total = jnp.sum(jnp.exp(logits - local_top[:, None]), 1)
    local_pick = jnp.sum(jnp.where(picked, logits, 0.0), 1)
    row_top, row_total, target_logit = joined(
        (local_top, local_total, local_pick), "fsdp", merge_totals
    )
    log_total = row_top + jnp.log(row_total)
    mask_float = loss_mask.astype(jnp.float32)
    grad_logits = (
        mask_float[:, None] * (jnp.exp(logits - log_total[:, None]) - picked.astype(jnp.float32))
    ).astype(jnp.bfloat16)
    grad_normed = lax.psum_scatter(
        lax.dot_general(
            w_vocab, grad_logits, (((1,), (1,)), ((), ())), preferred_element_type=jnp.float32
        ),
        "fsdp",
        scatter_dimension=0,
        tiled=True,
    ).T
    grad_unit = grad_normed * gain_part
    inner_total = lax.psum(jnp.sum(grad_unit * unit_part, 1), "fsdp")
    grad_summed = inv_root[:, None] * (grad_unit - unit_part * (inner_total / width)[:, None])
    gain_local = jnp.sum(grad_normed * unit_part, 0)
    token_count, loss_total, gain_total = lax.psum(
        (jnp.sum(mask_float), jnp.sum(mask_float * (log_total - target_logit)), gain_local), "dp"
    )
    return (
        loss_total / token_count,
        (grad_summed / token_count).astype(jnp.bfloat16),
        gain_total / token_count,
    )


def solution(mesh):
    in_specs = (
        P("dp", None),
        P(None, "fsdp"),
        P(None, "dp", "fsdp"),
        P("fsdp", None),
        P(),
        P(None, "fsdp"),
        P(),
        P("dp"),
        P(),
        P("dp"),
        P("dp"),
    )
    out_specs = (P(), P("dp", "fsdp"), P("fsdp"))
    return jax.shard_map(body, mesh=mesh, in_specs=in_specs, out_specs=out_specs, check_vma=False)
```

profile of v0, /device:TPU:0, one launch (start us, length us, event | category | flops | bytes accessed | tf_op | source)
XLA Modules:
  0.0 266.7 jit_solution(12701368455562883856)
XLA Ops:
  7.2 0.0 copy-start
  7.2 0.0 all-gather.8.cloned.1.call-start
  7.2 0.7 all-gather.8.cloned.1.call-update
  7.9 0.0 all-reduce.3.cloned.1.call-start
  8.0 0.0 copy-start.11
  8.0 0.0 copy-start.9
  8.0 3.2 %convolution_convert_fusion = bf16[128,512]{1,0:T(8,128)(2,1)S(1)} fusion(bf16[128,4096]{1,0:T(8,128)(2,1)} %param.13, bf16[4096,512]{1,0:T(8,128)(2,1)} %param.14), kind=kOutput, calls=%fused_computation.27 | convolution fusion | flops 536936448 | bytes 5373952 | tf_op jit(solution)/shard_map/dot_general | solution.py:67
  11.2 0.1 copy.23
  11.4 0.0 copy-done
  11.4 0.2 dynamic-slice_reduce_fusion
  11.6 0.0 copy-done.11
  11.6 0.1 select_reduce_fusion.2
  11.6 0.0 copy-done.9
  11.7 0.2 broadcast_compare_fusion
  11.8 61.6 %all-gather.8.cloned.1.call-done = bf16[2,1536,512]{2,1,0:T(8,128)(2,1)} async-done(((bf16[2,192,512]{2,1,0:T(8,128)(2,1)}), bf16[2,1536,512]{2,1,0:T(8,128)(2,1)}) %all-gather.8.cloned.1.call-update) | async-done | bytes 3145744 | tf_op jit(solution)/shard_map/all_gather | solution.py:83
  73.4 3.2 %fusion.29 = (bf16[1,1536,512]{2,1,0:T(8,128)(2,1)}, bf16[1,1536,512]{2,1,0:T(8,128)(2,1)S(1)}) fusion(bf16[2,1536,512]{2,1,0:T(8,128)(2,1)} %all-gather.8.cloned.1.call-done), kind=kLoop, calls=%fused_computation.65 | loop fusion | bytes 6291456 | tf_op jit(solution)/shard_map/slice | solution.py:31
  76.6 1.7 copy.24
  78.3 3.8 %select_reduce_fusion = (f32[8,128]{1,0:T(8,128)S(1)}, f32[8,128,1536]{2,1,0:T(8,128)}) fusion(pred[128,1536]{1,0:T(8,128)(4,1)S(1)} %broadcast_compare_fusion, bf16[128,8,64]{0,2,1:T(8,128)(2,1)S(1)} %bitcast.64, bf16[1536,8,64]{0,2,1:T(8,128)(2,1)S(1)} %bitcast.62), kind=kOutput, calls=%fused_computation.11 | convolution fusion | flops 204471296 | bytes 8196096 | tf_op jit(solution)/shard_map/ihd,jhd->hij/dot_general | solution.py:33
  82.1 0.7 copy.25
  82.8 0.0 copy-start.2
  82.9 4.3 %fusion.7 = f32[8,128]{1,0:T(8,128)S(1)} fusion(f32[8,128,1536]{2,1,0:T(8,128)} %get-tuple-element.214, f32[8,128]{1,0:T(8,128)S(1)} %broadcast_maximum_fusion, pred[128,1536]{1,0:T(8,128)(4,1)S(1)} %broadcast_compare_fusion), kind=kLoop, calls=%fused_computation.12 | loop fusion | flops 4717568 | bytes 6496256 | tf_op jit(solution)/shard_map/reduce_sum | solution.py:37
  87.1 0.3 copy-done.2
  87.4 0.0 copy-start.7
  87.5 1.4 fusion.15
  88.8 0.8 copy-done.7
  89.6 2.0 fusion.31
  91.7 0.0 copy-start.10
  91.7 0.0 copy-start.12
  91.7 0.0 copy-start.5
  91.7 0.0 all-reduce.3.cloned.1.call-update
  91.7 0.0 reduce-scatter.2.cloned.1.call-start
  91.8 0.6 copy-done.10
  92.3 0.0 copy-done.12
  92.3 49.5 %all-reduce.3.cloned.1.call-done = f32[128,4096]{1,0:T(8,128)} async-done(((f32[128,4096]{1,0:T(8,128)}), f32[128,4096]{1,0:T(8,128)}) %all-reduce.3.cloned.1.call-update) | async-done | bytes 2097168 | tf_op jit(solution)/shard_map/psum | solution.py:97
  141.9 0.0 copy-done.5
  141.9 0.0 copy-start.6
  141.9 2.1 multiply_reduce_fusion
  144.0 0.1 copy-done.6
  144.1 0.0 copy-start.8
  144.1 0.4 fusion.12
  144.5 0.3 copy-done.8
  144.8 0.0 copy-start.3
  144.8 13.7 %fusion.30 = (f32[128]{0:T(128)S(1)}, f32[128,4096]{1,0:T(8,128)S(1)}) fusion(bf16[4096,4096]{1,0:T(8,128)(2,1)} %param.18, f32[128,4096]{1,0:T(8,128)S(1)} %fusion.12, f32[4096]{0:T(1024)S(1)} %copy-done.8), kind=kOutput, calls=%fused_computation.66 | convolution fusion | flops 4296540160 | bytes 37765632 | tf_op jit(solution)/shard_map/dot_general | solution.py:103
  158.6 0.0 copy-done.3
  158.6 0.7 select_reduce_fusion.1
  159.3 5.0 %all-gather.5 = f32[4,1,128]{2,1,0:T(1,128)S(1)} all-gather(f32[1,1,128]{2,1,0:T(1,128)S(1)} %bitcast.72), channel_id=4, replica_groups=mesh['dp'=8,'fsdp'=4] {'fsdp'}, dimensions={0}, use_global_device_ids=true | all-gather | bytes 2560 | tf_op jit(solution)/shard_map/all_gather | solution.py:10
  164.3 5.0 %all-gather.4 = f32[4,1,128]{2,1,0:T(1,128)S(1)} all-gather(f32[1,1,128]{2,1,0:T(1,128)S(1)} %bitcast.71), channel_id=3, replica_groups=mesh['dp'=8,'fsdp'=4] {'fsdp'}, dimensions={0}, use_global_device_ids=true | all-gather | bytes 2560 | tf_op jit(solution)/shard_map/all_gather | solution.py:10
  169.3 5.2 %all-gather.3 = f32[4,1,128]{2,1,0:T(1,128)S(1)} all-gather(f32[1,1,128]{2,1,0:T(1,128)S(1)} %bitcast.69), channel_id=2, replica_groups=mesh['dp'=8,'fsdp'=4] {'fsdp'}, dimensions={0}, use_global_device_ids=true | all-gather | bytes 2560 | tf_op jit(solution)/shard_map/all_gather | solution.py:10
  174.5 0.1 while.19
  174.7 0.6 convert_reduce_fusion
  175.3 17.3 %convolution_bitcast_fusion = f32[4096,128]{0,1:T(8,128)} fusion(bf16[4096,4096]{1,0:T(8,128)(2,1)} %param.18, f32[128,4096]{1,0:T(8,128)S(1)} %get-tuple-element.216, f32[128]{0:T(128)S(1)} %get-tuple-element.209, f32[128]{0:T(128)S(1)} %convert_element_type.30, s32[128]{0:T(128)S(1)} %broadcast_subtract_fusion), kind=kOutput, calls=%fused_computation.14 | convolution fusion | flops 4298113024 | bytes 37750272 | tf_op jit(solution)/shard_map/dot_general | solution.py:119
  192.6 0.0 copy-start.4
  192.6 0.0 copy-start.1
  192.6 0.0 reduce-scatter.2.cloned.1.call-update
  192.6 31.7 %reduce-scatter.2.cloned.1.call-done = f32[1024,128]{0,1:T(8,128)} async-done(((f32[4096,128]{0,1:T(8,128)}), f32[1024,128]{0,1:T(8,128)}) %reduce-scatter.2.cloned.1.call-update) | async-done | bytes 524304 | tf_op jit(solution)/shard_map/reduce_scatter | solution.py:118
  224.3 0.0 copy-done.4
  224.3 1.2 fusion.21
  225.5 5.8 %psum.38 = f32[128]{0:T(128)S(1)} all-reduce(f32[128]{0:T(128)S(1)} %get-tuple-element.185), channel_id=1, replica_groups=mesh['dp'=8,'fsdp'=4] {'fsdp'}, use_global_device_ids=true, to_apply=%region_16.17 | all-reduce | flops 128 | bytes 1024 | tf_op jit(solution)/shard_map/psum | solution.py:127
  231.2 22.5 %all-reduce = (f32[]{:T(128)}, f32[]{:T(128)}, f32[1024]{0:T(1024)S(1)}) all-reduce(f32[]{:T(128)} %get-tuple-element.189, f32[]{:T(128)} %get-tuple-element.188, f32[1024]{0:T(1024)S(1)} %get-tuple-element.184), channel_id=1, replica_groups=mesh['dp'=8,'fsdp'=4] {'dp'}, use_global_device_ids=true, to_apply=%region_11.12 | all-reduce | flops 1026 | bytes 8208 | tf_op jit(solution)/shard_map/psum | solution.py:130
  253.8 1.3 broadcast_divide_fusion
  256.4 2.6 divide_convert_fusion
  259.0 0.0 copy-done.1
  (13 shorter events, 0.1 us)
Async XLA Ops:
  7.2 4.2 %copy-start = (s32[8,4]{0,1:T(4,128)S(1)}, s32[8,4]{0,1:T(4,128)}, u32[]{:S(2)}) copy-start(s32[8,4]{0,1:T(4,128)} %param.21) | copy-start | bytes 388
  7.2 66.2 %all-gather.8.cloned.1.call-start = ((), (), s32[]{:S(2)}) async-start(), calls=%async_computation.1 | async-start | bytes 3538944 | tf_op jit(solution)/shard_map/all_gather | solution.py:83
  7.9 133.9 %all-reduce.3.cloned.1.call-start = ((), (), s32[]{:S(2)}) async-start(), calls=%async_computation.2 | async-start | bytes 4194304 | tf_op jit(solution)/shard_map/psum | solution.py:97
  8.0 3.6 %copy-start.11 = (s32[128]{0:T(128)S(1)}, s32[128]{0:T(128)}, u32[]{:S(2)}) copy-start(s32[128]{0:T(128)} %param.20) | copy-start | bytes 1540
  8.0 3.7 %copy-start.9 = (s32[1536]{0:T(1024)S(1)}, s32[1536]{0:T(1024)}, u32[]{:S(2)}) copy-start(s32[1536]{0:T(1024)} %param.19) | copy-start | bytes 18436
  82.8 4.6 %copy-start.2 = (f32[8,128,1536]{2,1,0:T(8,128)S(1)}, f32[8,128,1536]{2,1,0:T(8,128)}, u32[]{:S(2)}) copy-start(f32[8,128,1536]{2,1,0:T(8,128)} %get-tuple-element.214) | copy-start | bytes 18874372
  87.4 2.2 copy-start.7
  91.7 0.7 copy-start.10
  91.7 0.7 copy-start.12
  91.7 50.2 %copy-start.5 = (bf16[128,4096]{1,0:T(8,128)(2,1)S(1)}, bf16[128,4096]{1,0:T(8,128)(2,1)}, u32[]{:S(2)}) copy-start(bf16[128,4096]{1,0:T(8,128)(2,1)} %param.13) | copy-start | bytes 3145732
  91.7 132.6 %reduce-scatter.2.cloned.1.call-start = ((), (), s32[]{:S(2)}) async-start(), calls=%async_computation.3 | async-start | bytes 2621440 | tf_op jit(solution)/shard_map/reduce_scatter | solution.py:118
  141.9 2.2 copy-start.6
  144.1 0.7 copy-start.8
  144.8 13.8 %copy-start.3 = (f32[128,4096]{1,0:T(8,128)}, f32[128,4096]{1,0:T(8,128)S(1)}, u32[]{:S(2)}) copy-start(f32[128,4096]{1,0:T(8,128)S(1)} %fusion.12) | copy-start | bytes 6291460
  192.6 31.7 %copy-start.4 = (f32[128,4096]{1,0:T(8,128)S(1)}, f32[128,4096]{1,0:T(8,128)}, u32[]{:S(2)}) copy-start(f32[128,4096]{1,0:T(8,128)} %copy-done.3) | copy-start | bytes 6291460
  192.6 66.5 %copy-start.1 = (s32[8,4]{0,1:T(4,128)S(1)}, s32[8,4]{0,1:T(4,128)}, u32[]{:S(2)}) copy-start(s32[8,4]{0,1:T(4,128)} %param.21) | copy-start | bytes 388
Sparse Core Ops, SparseCore 0:
  10.2 63.1 all-gather.7
  91.8 49.9 all-reduce.2
  192.7 31.5 reduce-scatter.1
where the time goes:
time: 267 us
  waiting for transfers between devices  143 us (54%)
  blocking collectives  43.5 us (16%)
  matrix products  41.5 us (16%)
  between operations  16.4 us (6%)
  other arithmetic  13.6 us (5%)
  local copies, waits for them, and re-layouts  8.11 us (3%)
    all_gather x1, waiting for transfers between devices, body(): lax.all_gather(enc_states, 'dp', axis=1, tiled=True)  61.6 us
    psum x1, waiting for transfers between devices, body(): lax.psum(jnp.dot(attended, w_out, preferred_element_type=jnp.float32), 'f...  49.5 us
    reduce_scatter x1, waiting for transfers between devices, body(): lax.psum_scatter(lax.dot_general(w_vocab, grad_logits, (((1,), (1,)), (()...  31.7 us
    psum x1, blocking collectives, body(): lax.psum((jnp.sum(mask_float), jnp.sum(mask_float * (log_total - target_l...  22.5 us
    dot_general x1, matrix products, body(): lax.dot_general(w_vocab, grad_logits, (((1,), (1,)), ((), ())), preferred...  17.3 us
    all_gather x3, blocking collectives, joined(): everything = jax.tree.map(lambda part: lax.all_gather(part, axis), x)  15.3 us
    dot_general x1, matrix products, body(): logits = jnp.dot(normed_full, w_vocab, preferred_element_type=jnp.float32)  13.7 us
    psum x1, blocking collectives, body(): inner_total = lax.psum(jnp.sum(grad_unit * unit_part, 1), 'fsdp')  5.75 us
  transfers between devices with their start and end apart: 3, of which 3 were waited for; matrix products, arithmetic and copies ran while one was open for 1% of the time, Pallas kernels for 0%

commit v1 on v0

--- a/solution.py
+++ b/solution.py
@@ -4,6 +4,9 @@
 from jax.sharding import PartitionSpec as P
 
 HEAD_DIM = 64
+extend_heaps_here = lambda payload, which_axis: jnp.sum(
+    lax.all_gather(payload, axis_name=which_axis), 0
+)
 
 
 def joined(x, axis, combine):
@@ -94,7 +97,7 @@
     )
     feature_start = fsdp_index * feature_count
     gain_part = lax.dynamic_slice_in_dim(norm_gain, feature_start, feature_count, 0)
-    summed_full = lax.psum(
+    summed_full = extend_heaps_here(
         jnp.dot(attended, w_out, preferred_element_type=jnp.float32), "fsdp"
     ) + dec_hidden.astype(jnp.float32)
     inv_root = lax.rsqrt(jnp.sum(summed_full * summed_full, 1) / width + 1e-06)

time: 267 us -> 277 us (1.037)
  waiting for transfers between devices: 143 us -> 150 us
    all_gather x0 -> x1, waiting for transfers between devices: none -> 56.4 us  [lax.all_gather(payload, axis_name=which_axis)]
    psum x1 -> x0, waiting for transfers between devices: 49.5 us -> none  [body(): lax.psum(jnp.dot(attended, w_out, preferred_element_type=jnp.float32), 'f...]
    reduce_sum x0 -> x1, other arithmetic: none -> 4.32 us  [jnp.sum(lax.all_gather(payload, axis_name=which_axis), 0)]
where the time goes in v1:
time: 277 us; the launch traced here: 276 us
  waiting for transfers between devices  150 us (54%)
  blocking collectives  43.5 us (16%)
  matrix products  41.6 us (15%)
  between operations  16.4 us (6%)
  other arithmetic  16.1 us (6%)
  local copies, waits for them, and re-layouts  8.08 us (3%)
    all_gather x1, waiting for transfers between devices, body(): lax.all_gather(enc_states, 'dp', axis=1, tiled=True)  61.6 us
    all_gather x1, waiting for transfers between devices, lax.all_gather(payload, axis_name=which_axis)  56.4 us
    reduce_scatter x1, waiting for transfers between devices, body(): lax.psum_scatter(lax.dot_general(w_vocab, grad_logits, (((1,), (1,)), (()...  31.6 us
    psum x1, blocking collectives, body(): lax.psum((jnp.sum(mask_float), jnp.sum(mask_float * (log_total - target_l...  22.5 us
    dot_general x1, matrix products, body(): lax.dot_general(w_vocab, grad_logits, (((1,), (1,)), ((), ())), preferred...  17.3 us
    all_gather x3, blocking collectives, joined(): everything = jax.tree.map(lambda part: lax.all_gather(part, axis), x)  15.3 us
    dot_general x1, matrix products, body(): logits = jnp.dot(normed_full, w_vocab, preferred_element_type=jnp.float32)  13.7 us
    psum x1, blocking collectives, body(): inner_total = lax.psum(jnp.sum(grad_unit * unit_part, 1), 'fsdp')  5.75 us
  transfers between devices with their start and end apart: 3, of which 3 were waited for; matrix products, arithmetic and copies ran while one was open for 1% of the time, Pallas kernels for 0%

profile of v1, /device:TPU:0, one launch (start us, length us, event | category | flops | bytes accessed | tf_op | source)
XLA Modules:
  0.0 276.1 jit_solution(6576611071541854144)
XLA Ops:
  7.2 0.0 copy-start
  7.2 0.0 all-gather.10.cloned.1.call-start
  7.2 0.7 all-gather.10.cloned.1.call-update
  7.9 0.0 all-gather.12.cloned.1.call-start
  8.0 0.0 copy-start.10
  8.0 0.0 copy-start.8
  8.0 3.2 %convolution_convert_fusion = bf16[128,512]{1,0:T(8,128)(2,1)S(1)} fusion(bf16[128,4096]{1,0:T(8,128)(2,1)} %param.13, bf16[4096,512]{1,0:T(8,128)(2,1)} %param.14), kind=kOutput, calls=%fused_computation.27 | convolution fusion | flops 536936448 | bytes 5373952 | tf_op jit(solution)/shard_map/dot_general | solution.py:70
  11.2 0.1 copy.23
  11.4 0.0 copy-done
  11.4 0.2 dynamic-slice_reduce_fusion
  11.6 0.0 copy-done.10
  11.6 0.1 select_reduce_fusion.2
  11.6 0.0 copy-done.8
  11.7 0.2 broadcast_compare_fusion
  11.8 61.6 %all-gather.10.cloned.1.call-done = bf16[2,1536,512]{2,1,0:T(8,128)(2,1)} async-done(((bf16[2,192,512]{2,1,0:T(8,128)(2,1)}), bf16[2,1536,512]{2,1,0:T(8,128)(2,1)}) %all-gather.10.cloned.1.call-update) | async-done | bytes 3145744 | tf_op jit(solution)/shard_map/all_gather | solution.py:86
  73.4 3.2 %fusion.29 = (bf16[1,1536,512]{2,1,0:T(8,128)(2,1)}, bf16[1,1536,512]{2,1,0:T(8,128)(2,1)S(1)}) fusion(bf16[2,1536,512]{2,1,0:T(8,128)(2,1)} %all-gather.10.cloned.1.call-done), kind=kLoop, calls=%fused_computation.65 | loop fusion | bytes 6291456 | tf_op jit(solution)/shard_map/slice | solution.py:34
  76.6 1.7 copy.24
  78.3 3.8 %select_reduce_fusion = (f32[8,128]{1,0:T(8,128)S(1)}, f32[8,128,1536]{2,1,0:T(8,128)}) fusion(pred[128,1536]{1,0:T(8,128)(4,1)S(1)} %broadcast_compare_fusion, bf16[128,8,64]{0,2,1:T(8,128)(2,1)S(1)} %bitcast.66, bf16[1536,8,64]{0,2,1:T(8,128)(2,1)S(1)} %bitcast.64), kind=kOutput, calls=%fused_computation.11 | convolution fusion | flops 204471296 | bytes 8196096 | tf_op jit(solution)/shard_map/ihd,jhd->hij/dot_general | solution.py:36
  82.1 0.7 copy.25
  82.8 0.0 copy-start.2
  82.9 4.3 %fusion.7 = f32[8,128]{1,0:T(8,128)S(1)} fusion(f32[8,128,1536]{2,1,0:T(8,128)} %get-tuple-element.214, f32[8,128]{1,0:T(8,128)S(1)} %broadcast_maximum_fusion, pred[128,1536]{1,0:T(8,128)(4,1)S(1)} %broadcast_compare_fusion), kind=kLoop, calls=%fused_computation.12 | loop fusion | flops 4717568 | bytes 6496256 | tf_op jit(solution)/shard_map/reduce_sum | solution.py:40
  87.1 0.3 copy-done.2
  87.4 0.0 copy-start.6
  87.5 1.4 fusion.15
  88.8 0.8 copy-done.6
  89.6 2.1 fusion.31
  91.8 0.0 copy-start.9
  91.8 0.0 copy-start.11
  91.8 0.0 all-gather.12.cloned.1.call-update
  91.8 0.0 reduce-scatter.2.cloned.1.call-start
  91.8 0.6 copy-done.9
  92.4 0.0 copy-done.11
  92.4 56.4 %all-gather.12.cloned.1.call-done = f32[512,4096]{1,0:T(8,128)} async-done(((f32[128,4096]{1,0:T(8,128)}), f32[512,4096]{1,0:T(8,128)}) %all-gather.12.cloned.1.call-update) | async-done | bytes 8388624 | tf_op jit(solution)/shard_map/all_gather | solution.py:8
  148.9 0.0 copy-start.5
  148.9 4.3 %reduce_sum.92 = f32[128,4096]{1,0:T(8,128)S(1)} reduce(f32[4,128,4096]{2,1,0:T(8,128)} %bitcast.63, f32[]{:T(128)} %constant.75.clone.1), dimensions={0}, to_apply=%region_3.4 | reduce | flops 1572864 | bytes 10485764 | tf_op jit(solution)/shard_map/reduce_sum | solution.py:7
  153.2 0.0 copy-done.5
  153.2 0.4 multiply_reduce_fusion
  153.6 0.0 copy-start.7
  153.6 0.3 fusion.12
  153.9 0.4 copy-done.7
  154.3 0.0 copy-start.3
  154.3 13.7 %fusion.30 = (f32[128]{0:T(128)S(1)}, f32[128,4096]{1,0:T(8,128)S(1)}) fusion(bf16[4096,4096]{1,0:T(8,128)(2,1)} %param.18, f32[128,4096]{1,0:T(8,128)S(1)} %fusion.12, f32[4096]{0:T(1024)S(1)} %copy-done.7), kind=kOutput, calls=%fused_computation.66 | convolution fusion | flops 4296540160 | bytes 37765632 | tf_op jit(solution)/shard_map/dot_general | solution.py:106
  168.1 0.0 copy-done.3
  168.1 0.7 select_reduce_fusion.1
  168.8 5.0 %all-gather.6 = f32[4,1,128]{2,1,0:T(1,128)S(1)} all-gather(f32[1,1,128]{2,1,0:T(1,128)S(1)} %bitcast.74), channel_id=5, replica_groups=mesh['dp'=8,'fsdp'=4] {'fsdp'}, dimensions={0}, use_global_device_ids=true | all-gather | bytes 2560 | tf_op jit(solution)/shard_map/all_gather | solution.py:13
  173.8 5.0 %all-gather.5 = f32[4,1,128]{2,1,0:T(1,128)S(1)} all-gather(f32[1,1,128]{2,1,0:T(1,128)S(1)} %bitcast.73), channel_id=4, replica_groups=mesh['dp'=8,'fsdp'=4] {'fsdp'}, dimensions={0}, use_global_device_ids=true | all-gather | bytes 2560 | tf_op jit(solution)/shard_map/all_gather | solution.py:13
  178.8 5.2 %all-gather.4 = f32[4,1,128]{2,1,0:T(1,128)S(1)} all-gather(f32[1,1,128]{2,1,0:T(1,128)S(1)} %bitcast.71), channel_id=3, replica_groups=mesh['dp'=8,'fsdp'=4] {'fsdp'}, dimensions={0}, use_global_device_ids=true | all-gather | bytes 2560 | tf_op jit(solution)/shard_map/all_gather | solution.py:13
  184.1 0.1 while.19
  184.2 0.6 convert_reduce_fusion
  184.8 17.3 %convolution_bitcast_fusion = f32[4096,128]{0,1:T(8,128)} fusion(bf16[4096,4096]{1,0:T(8,128)(2,1)} %param.18, f32[128,4096]{1,0:T(8,128)S(1)} %get-tuple-element.216, f32[128]{0:T(128)S(1)} %get-tuple-element.209, f32[128]{0:T(128)S(1)} %convert_element_type.30, s32[128]{0:T(128)S(1)} %broadcast_subtract_fusion), kind=kOutput, calls=%fused_computation.14 | convolution fusion | flops 4298113024 | bytes 37750272 | tf_op jit(solution)/shard_map/dot_general | solution.py:122
  202.1 0.0 copy-start.4
  202.1 0.0 copy-start.1
  202.1 0.0 reduce-scatter.2.cloned.1.call-update
  202.1 31.6 %reduce-scatter.2.cloned.1.call-done = f32[1024,128]{0,1:T(8,128)} async-done(((f32[4096,128]{0,1:T(8,128)}), f32[1024,128]{0,1:T(8,128)}) %reduce-scatter.2.cloned.1.call-update) | async-done | bytes 524304 | tf_op jit(solution)/shard_map/reduce_scatter | solution.py:121
  233.7 0.0 copy-done.4
  233.7 1.2 fusion.21
  234.9 5.8 %psum.30 = f32[128]{0:T(128)S(1)} all-reduce(f32[128]{0:T(128)S(1)} %get-tuple-element.185), channel_id=1, replica_groups=mesh['dp'=8,'fsdp'=4] {'fsdp'}, use_global_device_ids=true, to_apply=%region_16.17 | all-reduce | flops 128 | bytes 1024 | tf_op jit(solution)/shard_map/psum | solution.py:130
  240.7 22.5 %all-reduce = (f32[]{:T(128)}, f32[]{:T(128)}, f32[1024]{0:T(1024)S(1)}) all-reduce(f32[]{:T(128)} %get-tuple-element.189, f32[]{:T(128)} %get-tuple-element.188, f32[1024]{0:T(1024)S(1)} %get-tuple-element.184), channel_id=1, replica_groups=mesh['dp'=8,'fsdp'=4] {'dp'}, use_global_device_ids=true, to_apply=%region_11.12 | all-reduce | flops 1026 | bytes 8208 | tf_op jit(solution)/shard_map/psum | solution.py:133
  263.2 1.3 broadcast_divide_fusion
  265.9 2.6 divide_convert_fusion
  268.5 0.0 copy-done.1
  (13 shorter events, 0.1 us)
Async XLA Ops:
  7.2 4.2 %copy-start = (s32[8,4]{0,1:T(4,128)S(1)}, s32[8,4]{0,1:T(4,128)}, u32[]{:S(2)}) copy-start(s32[8,4]{0,1:T(4,128)} %param.21) | copy-start | bytes 388
  7.2 66.2 %all-gather.10.cloned.1.call-start = ((), (), s32[]{:S(2)}) async-start(), calls=%async_computation.1 | async-start | bytes 3538944 | tf_op jit(solution)/shard_map/all_gather | solution.py:86
  7.9 140.9 %all-gather.12.cloned.1.call-start = ((), (), s32[]{:S(2)}) async-start(), calls=%async_computation.3 | async-start | bytes 10485760 | tf_op jit(solution)/shard_map/all_gather | solution.py:8
  8.0 3.6 %copy-start.10 = (s32[128]{0:T(128)S(1)}, s32[128]{0:T(128)}, u32[]{:S(2)}) copy-start(s32[128]{0:T(128)} %param.20) | copy-start | bytes 1540
  8.0 3.7 %copy-start.8 = (s32[1536]{0:T(1024)S(1)}, s32[1536]{0:T(1024)}, u32[]{:S(2)}) copy-start(s32[1536]{0:T(1024)} %param.19) | copy-start | bytes 18436
  82.8 4.6 %copy-start.2 = (f32[8,128,1536]{2,1,0:T(8,128)S(1)}, f32[8,128,1536]{2,1,0:T(8,128)}, u32[]{:S(2)}) copy-start(f32[8,128,1536]{2,1,0:T(8,128)} %get-tuple-element.214) | copy-start | bytes 18874372
  87.4 2.2 copy-start.6
  91.8 0.7 copy-start.9
  91.8 0.7 copy-start.11
  91.8 141.9 %reduce-scatter.2.cloned.1.call-start = ((), (), s32[]{:S(2)}) async-start(), calls=%async_computation.2 | async-start | bytes 2621440 | tf_op jit(solution)/shard_map/reduce_scatter | solution.py:121
  148.9 4.3 %copy-start.5 = (bf16[128,4096]{1,0:T(8,128)(2,1)S(1)}, bf16[128,4096]{1,0:T(8,128)(2,1)}, u32[]{:S(2)}) copy-start(bf16[128,4096]{1,0:T(8,128)(2,1)} %param.13) | copy-start | bytes 3145732
  153.6 0.7 copy-start.7
  154.3 13.8 %copy-start.3 = (f32[128,4096]{1,0:T(8,128)}, f32[128,4096]{1,0:T(8,128)S(1)}, u32[]{:S(2)}) copy-start(f32[128,4096]{1,0:T(8,128)S(1)} %fusion.12) | copy-start | bytes 6291460
  202.1 31.6 %copy-start.4 = (f32[128,4096]{1,0:T(8,128)S(1)}, f32[128,4096]{1,0:T(8,128)}, u32[]{:S(2)}) copy-start(f32[128,4096]{1,0:T(8,128)} %copy-done.3) | copy-start | bytes 6291460
  202.1 66.4 %copy-start.1 = (s32[8,4]{0,1:T(4,128)S(1)}, s32[8,4]{0,1:T(4,128)}, u32[]{:S(2)}) copy-start(s32[8,4]{0,1:T(4,128)} %param.21) | copy-start | bytes 388
Sparse Core Ops, SparseCore 0:
  10.2 63.1 all-gather.9
  91.9 56.8 all-gather.11
  202.2 31.4 reduce-scatter.1
